TPU v7x, 256 devices: a whole 4x4x8 slice. The times are simulated.
256 devices in a mesh: gx: 8 (over x, core), gy: 8 (over z), gz: 4 (over y).
Axes of the slice: x: 4, y: 4, z: 8, core: 2. Of those that a mesh axis runs over, the one named last changes fastest.
Arguments:
- orbitals: float32 [32, 64, 128, 512], P(None, 'gx', 'gy', 'gz'), may hold values from -12 to 12
- potential: float32 [64, 128, 512], P('gx', 'gy', 'gz'), may hold values from -1 to 1
Outputs:
- filtered_basis: float32 [32, 64, 128, 512], P(None, 'gx', 'gy', 'gz')
- r_factor: float32 [32, 32], replicated
All inputs are finite; a program needn't handle non-finite values.
Results may differ from a plain program's by a relative error of at most 0.00013.
Values sent between devices are 32-bit elements; how exact they have to be, the bound alone decides.
No kernel may reach another device: no remote copies, remote signals or barrier semaphores. Data moves between devices by JAX's collectives and lax.ppermute only.
A program may use at most 128 MiB of HBM per device.

v0:
```python
import jax
import jax.numpy as jnp
from jax import lax
from jax.sharding import PartitionSpec as P

TAPS = (-1.0 / 12.0, 4.0 / 3.0, -2.5, 4.0 / 3.0, -1.0 / 12.0)


def padded_2(x, sides, width):
    for axis, dim in sides:
        devices, length = (lax.axis_size(axis), x.shape[dim])
        up = [(i, (i + 1) % devices) for i in range(devices)]
        down = [(j, i) for i, j in up]
        last = lax.slice_in_dim(x, length - width, length, axis=dim)
        leading = lax.slice_in_dim(x, 0, width, axis=dim)
        before = lax.ppermute(last, axis, up)
        after = lax.ppermute(leading, axis, down)
        x = jnp.concatenate([before, x, after], axis=dim)
    return x


def window(padded, shift_x, shift_y, shift_z):
    sizes = padded.shape
    return padded[
        :,
        2 + shift_x : sizes[1] - 2 + shift_x,
        2 + shift_y : sizes[2] - 2 + shift_y,
        2 + shift_z : sizes[3] - 2 + shift_z,
    ]


def laplacian(padded):
    summed = 3.0 * TAPS[2] * window(padded, 0, 0, 0)
    for offset, weight in ((-2, TAPS[0]), (-1, TAPS[1]), (1, TAPS[3]), (2, TAPS[4])):
        summed = summed + weight * window(padded, offset, 0, 0)
        summed = summed + weight * window(padded, 0, offset, 0)
        summed = summed + weight * window(padded, 0, 0, offset)
    return summed


def hamiltonian(padded, potential_core):
    return -0.5 * laplacian(padded) + potential_core * window(padded, 0, 0, 0)


def with_rims(field):
    return padded_2(field, (("gx", 1), ("gy", 2), ("gz", 3)), 2)


def per_device(orbitals, potential):
    potential_cube = potential[None]
    first = (hamiltonian(with_rims(orbitals), potential_cube) - 5.5 * orbitals) / 3.5
    second = 2.0 * (hamiltonian(with_rims(first), potential_cube) - 5.5 * first) / 3.5 - orbitals
    norb_count = orbitals.shape[0]
    filtered = second.reshape(norb_count, -1)
    all_cells = filtered.shape[1] * lax.axis_size("gx") * lax.axis_size("gy") * lax.axis_size("gz")
    correlation = jnp.dot(filtered, filtered.T, precision=lax.Precision.HIGHEST) / all_cells
    lower = jnp.linalg.cholesky(lax.psum(correlation, ("gx", "gy", "gz")))
    basis = jax.scipy.linalg.solve_triangular(lower, filtered, lower=True)
    return (basis.reshape(orbitals.shape), lower.T)


def solution(mesh):
    in_specs = (P(None, "gx", "gy", "gz"), P("gx", "gy", "gz"))
    out_specs = (P(None, "gx", "gy", "gz"), P())
    return jax.shard_map(
        per_device, mesh=mesh, in_specs=in_specs, out_specs=out_specs, check_vma=False
    )
```

profile of v0, /device:TPU:1, one launch (start us, length us, event | category | flops | bytes accessed | tf_op | source)
XLA Modules:
  0.0 230.9 jit_solution(3430019254784717829)
XLA Ops:
  2.2 2.6 %collective-permute-start = (f32[32,2,16,128]{3,0,2,1:T(8,128)S(1)}, f32[32,2,16,128]{3,0,2,1:T(8,128)S(1)}, u32[]{:S(2)}, u32[]{:S(2)}) collective-permute-start(f32[32,2,16,128]{3,0,2,1:T(8,128)S(1)} %copy.80), channel_id=1, source_target_pairs={{0,32},{32,64},{64,96},{96,128},{128,160},{160,192},{192,224},{224... | collective-permute-start | bytes 1572872 | tf_op jit(solution)/shard_map/ppermute | solution.py:16
  5.8 5.2 %collective-permute-done = f32[32,2,16,128]{3,0,2,1:T(8,128)S(1)} collective-permute-done((f32[32,2,16,128]{3,0,2,1:T(8,128)S(1)}, f32[32,2,16,128]{3,0,2,1:T(8,128)S(1)}, u32[]{:S(2)}, u32[]{:S(2)}) %collective-permute-start) | collective-permute-done | bytes 524320 | tf_op jit(solution)/shard_map/ppermute | solution.py:16
  15.6 4.0 %collective-permute-start.3 = (f32[32,12,2,128]{3,0,2,1:T(8,128)S(1)}, f32[32,12,2,128]{3,0,2,1:T(8,128)S(1)}, u32[]{:S(2)}, u32[]{:S(2)}) collective-permute-start(f32[32,12,2,128]{3,0,2,1:T(8,128)S(1)} %get-tuple-element.21), channel_id=1, source_target_pairs={{4,0},{8,4},{12,8},{16,12},{20,16},{24,20},{28,24},{0,28},{5,1},{9... | collective-permute-start | bytes 1179656 | tf_op jit(solution)/shard_map/ppermute | solution.py:17
  19.7 8.1 %collective-permute-done.2 = f32[32,12,2,128]{3,0,2,1:T(8,128)S(1)} collective-permute-done((f32[32,12,2,128]{3,0,2,1:T(8,128)S(1)}, f32[32,12,2,128]{3,0,2,1:T(8,128)S(1)}, u32[]{:S(2)}, u32[]{:S(2)}) %collective-permute-start.2) | collective-permute-done | bytes 393248 | tf_op jit(solution)/shard_map/ppermute | solution.py:16
  28.2 4.7 %fusion.56 = (f32[32,12,20,2]{3,0,2,1:T(8,128)}, f32[32,12,20,2]{3,0,2,1:T(8,128)}) fusion(f32[32,12,20,128]{3,0,2,1:T(8,128)S(1)} %pad_maximum_fusion), kind=kLoop, calls=%fused_computation.120 | loop fusion | bytes 245760 | tf_op jit(solution)/shard_map/slice | solution.py:14
  32.9 3.4 %copy.47 = f32[32,12,20,2]{0,2,3,1:T(8,128)S(1)} copy(f32[32,12,20,2]{3,0,2,1:T(8,128)} %get-tuple-element.14) | data formatting | bytes 122880 | tf_op jit(solution)/shard_map/slice | solution.py:14
  37.6 3.4 %copy.50 = f32[32,12,20,2]{0,2,3,1:T(8,128)S(1)} copy(f32[32,12,20,2]{3,0,2,1:T(8,128)} %get-tuple-element.15) | data formatting | bytes 122880 | tf_op jit(solution)/shard_map/slice | solution.py:15
  41.0 1.7 collective-permute-start.5
  42.7 1.6 collective-permute-done.4
  44.3 2.9 %copy.48 = f32[32,12,20,2]{3,0,2,1:T(8,128)} copy(f32[32,12,20,2]{0,2,3,1:T(8,128)S(1)} %collective-permute-done.4) | data formatting | bytes 122880 | tf_op jit(solution)/shard_map/ppermute | solution.py:16
  47.7 2.9 %copy.51 = f32[32,12,20,2]{3,0,2,1:T(8,128)} copy(f32[32,12,20,2]{0,2,3,1:T(8,128)S(1)} %collective-permute-done.5) | data formatting | bytes 122880 | tf_op jit(solution)/shard_map/ppermute | solution.py:17
  50.5 17.0 %broadcast_multiply_fusion = (f32[32,8,16,128]{3,0,2,1:T(8,128)S(1)}, f32[32,8,16,128]{3,0,2,1:T(8,128)}) fusion(f32[8,16,128]{2,1,0:T(8,128)S(1)} %copy-done.5, f32[32,12,20,2]{3,0,2,1:T(8,128)} %copy.51, f32[32,12,2,128]{3,0,2,1:T(8,128)S(1)} %collective-permute-done.3, f32[32,12,16,128]{3,0,2,1:T(8,128)} %copy-done.1, ...), kind=kLoop, calls=%fused_computation.97 | loop fusion | flops 24641536 | bytes 18800640 | tf_op jit(solution)/shard_map/div | solution.py:51
  67.6 5.3 %collective-permute-start.6 = (f32[32,2,16,128]{3,0,2,1:T(8,128)S(1)}, f32[32,2,16,128]{3,0,2,1:T(8,128)S(1)}, u32[]{:S(2)}, u32[]{:S(2)}) collective-permute-start(f32[32,2,16,128]{3,0,2,1:T(8,128)S(1)} %get-tuple-element.22), channel_id=1, source_target_pairs={{0,32},{32,64},{64,96},{96,128},{128,160},{160,192},{192,224},{224... | collective-permute-start | bytes 1572872 | tf_op jit(solution)/shard_map/ppermute | solution.py:16
  72.9 6.1 %collective-permute-done.6 = f32[32,2,16,128]{3,0,2,1:T(8,128)S(1)} collective-permute-done((f32[32,2,16,128]{3,0,2,1:T(8,128)S(1)}, f32[32,2,16,128]{3,0,2,1:T(8,128)S(1)}, u32[]{:S(2)}, u32[]{:S(2)}) %collective-permute-start.6) | collective-permute-done | bytes 524320 | tf_op jit(solution)/shard_map/ppermute | solution.py:16
  79.1 2.5 %collective-permute-done.7 = f32[32,2,16,128]{3,0,2,1:T(8,128)S(1)} collective-permute-done((f32[32,2,16,128]{3,0,2,1:T(8,128)S(1)}, f32[32,2,16,128]{3,0,2,1:T(8,128)S(1)}, u32[]{:S(2)}, u32[]{:S(2)}) %collective-permute-start.7) | collective-permute-done | bytes 524320 | tf_op jit(solution)/shard_map/ppermute | solution.py:17
  81.7 2.7 %collective-permute-start.9 = (f32[32,12,2,128]{3,0,2,1:T(8,128)S(1)}, f32[32,12,2,128]{3,0,2,1:T(8,128)S(1)}, u32[]{:S(2)}, u32[]{:S(2)}) collective-permute-start(f32[32,12,2,128]{3,0,2,1:T(8,128)S(1)} %get-tuple-element.19), channel_id=1, source_target_pairs={{4,0},{8,4},{12,8},{16,12},{20,16},{24,20},{28,24},{0,28},{5,1},{9... | collective-permute-start | bytes 1179656 | tf_op jit(solution)/shard_map/ppermute | solution.py:17
  85.0 8.1 %collective-permute-done.8 = f32[32,12,2,128]{3,0,2,1:T(8,128)S(1)} collective-permute-done((f32[32,12,2,128]{3,0,2,1:T(8,128)S(1)}, f32[32,12,2,128]{3,0,2,1:T(8,128)S(1)}, u32[]{:S(2)}, u32[]{:S(2)}) %collective-permute-start.8) | collective-permute-done | bytes 393248 | tf_op jit(solution)/shard_map/ppermute | solution.py:16
  94.0 4.7 %fusion.55 = (f32[32,12,20,2]{3,0,2,1:T(8,128)}, f32[32,12,20,2]{3,0,2,1:T(8,128)}) fusion(f32[32,12,20,128]{3,0,2,1:T(8,128)S(1)} %pad_maximum_fusion.1), kind=kLoop, calls=%fused_computation.119 | loop fusion | bytes 245760 | tf_op jit(solution)/shard_map/slice | solution.py:14
  98.6 4.0 %copy.54 = f32[32,12,20,2]{0,2,3,1:T(8,128)} copy(f32[32,12,20,2]{3,0,2,1:T(8,128)} %get-tuple-element.12) | data formatting | bytes 122880 | tf_op jit(solution)/shard_map/slice | solution.py:14
  102.7 4.0 %copy.56 = f32[32,12,20,2]{0,2,3,1:T(8,128)} copy(f32[32,12,20,2]{3,0,2,1:T(8,128)} %get-tuple-element.13) | data formatting | bytes 122880 | tf_op jit(solution)/shard_map/slice | solution.py:15
  106.7 2.7 %collective-permute-start.11 = (f32[32,12,20,2]{0,2,3,1:T(8,128)}, f32[32,12,20,2]{0,2,3,1:T(8,128)}, u32[]{:S(2)}, u32[]{:S(2)}) collective-permute-start(f32[32,12,20,2]{0,2,3,1:T(8,128)} %copy.56), channel_id=1, source_target_pairs={{1,0},{2,1},{3,2},{0,3},{5,4},{6,5},{7,6},{4,7},{9,8},{10,9},{11,1... | collective-permute-start | bytes 184328 | tf_op jit(solution)/shard_map/ppermute | solution.py:17
  109.4 4.3 %maximum_maximum_fusion = (f32[32,12,18,128]{3,0,2,1:T(8,128)}, f32[32,12,18,128]{3,0,2,1:T(8,128)}) fusion(f32[32,2,16,128]{3,0,2,1:T(8,128)S(1)} %collective-permute-done.7, f32[32,8,16,128]{3,0,2,1:T(8,128)S(1)} %get-tuple-element.10, f32[32,2,16,128]{3,0,2,1:T(8,128)S(1)} %collective-permute-done.6, f32[32,12,2,128]{3,0,2,1:T(8,128)S(1)} %collective-permute-done.8, ...), kind=kLoop, calls=%fused_computation.6 | loop fusion | flops 5308416 | bytes 11010048 | tf_op jit(solution)/shard_map/concatenate | solution.py:18
  113.7 5.4 %collective-permute-done.10 = f32[32,12,20,2]{0,2,3,1:T(8,128)} collective-permute-done((f32[32,12,20,2]{0,2,3,1:T(8,128)}, f32[32,12,20,2]{0,2,3,1:T(8,128)}, u32[]{:S(2)}, u32[]{:S(2)}) %collective-permute-start.10) | collective-permute-done | bytes 61472 | tf_op jit(solution)/shard_map/ppermute | solution.py:16
  119.1 3.7 %copy.55 = f32[32,12,20,2]{3,0,2,1:T(8,128)} copy(f32[32,12,20,2]{0,2,3,1:T(8,128)} %collective-permute-done.10) | data formatting | bytes 122880 | tf_op jit(solution)/shard_map/ppermute | solution.py:16
  122.9 3.8 %copy.57 = f32[32,12,20,2]{3,0,2,1:T(8,128)} copy(f32[32,12,20,2]{0,2,3,1:T(8,128)} %collective-permute-done.11) | data formatting | bytes 122880 | tf_op jit(solution)/shard_map/ppermute | solution.py:17
  126.6 9.9 %fusion.12 = f32[32,8,16,128]{3,0,2,1:T(8,128)S(1)} fusion(f32[32,8,16,128]{3,0,2,1:T(8,128)S(1)} %get-tuple-element.10, f32[32,2,16,128]{3,0,2,1:T(8,128)S(1)} %collective-permute-done.7, f32[32,2,16,128]{3,0,2,1:T(8,128)S(1)} %collective-permute-done.6, f32[32,12,20,2]{3,0,2,1:T(8,128)} %copy.57, f32[32,12,2,128]{3,0,2,1:T(8,128)} %copy-done.4, ...), kind=kLoop, calls=%fused_computation.24 | loop fusion | flops 29360128 | bytes 18800640 | tf_op jit(solution)/shard_map/sub | solution.py:52
  136.5 1.8 fusion.50
  139.5 76.7 %psum.7 = f32[32,32]{0,1:T(8,128)S(1)} all-reduce(f32[32,32]{0,1:T(8,128)S(1)} %fusion.50), channel_id=1, replica_groups=mesh['gx'=8,'gy'=8,'gz'=4] {'gx','gy','gz'}, use_global_device_ids=true, to_apply=%region_0.0 | all-reduce | flops 1024 | bytes 8192 | tf_op jit(solution)/shard_map/psum | solution.py:57
  217.9 2.9 %cholesky.16 = f32[32,32]{1,0:T(8,128)S(1)} custom-call(f32[32,32]{1,0:T(8,128)S(1)} %fusion.52), custom_call_target="Cholesky" | custom-call | tf_op jit(solution)/shard_map/jit(cholesky)/cholesky | solution.py:57
  222.8 2.4 %custom-call.7 = f32[1,32,32]{1,2,0:T(8,128)S(1)} custom-call(f32[1,32,32]{2,1,0:T(8,128)S(1)} %get-tuple-element.34), custom_call_target="InvertDiagBlocksLowerTriangular" | custom-call | tf_op jit(solution)/shard_map/jit(_solve_triangular)/triangular_solve | solution.py:58
  225.3 3.0 %fusion.48 = f32[32,8,16,128]{3,0,2,1:T(8,128)S(1)} fusion(f32[8,16,128,32]{2,1,0,3:T(8,128)S(1)} %bitcast.32, f32[1,32,32]{1,2,0:T(8,128)S(1)} %custom-call.7), kind=kOutput, calls=%fused_computation.93 | convolution fusion | flops 201326592 | bytes 4198400 | tf_op jit(solution)/shard_map/jit(_solve_triangular)/triangular_solve | solution.py:58
  228.3 2.5 %copy.64 = f32[32,8,16,128]{3,2,1,0:T(8,128)} copy(f32[32,8,16,128]{3,0,2,1:T(8,128)S(1)} %fusion.48) | data formatting | bytes 4194304
  (46 shorter events, 16.0 us)
Async XLA Ops:
  1.9 9.2 %copy-start = (f32[32,8,16,128]{3,2,1,0:T(8,128)S(1)}, f32[32,8,16,128]{3,2,1,0:T(8,128)}, u32[]{:S(2)}) copy-start(f32[32,8,16,128]{3,2,1,0:T(8,128)} %param.2) | copy-start | bytes 6291460
  2.2 8.7 %collective-permute-start = (f32[32,2,16,128]{3,0,2,1:T(8,128)S(1)}, f32[32,2,16,128]{3,0,2,1:T(8,128)S(1)}, u32[]{:S(2)}, u32[]{:S(2)}) collective-permute-start(f32[32,2,16,128]{3,0,2,1:T(8,128)S(1)} %copy.80), channel_id=1, source_target_pairs={{0,32},{32,64},{64,96},{96,128},{128,160},{160,192},{192,224},{224... | collective-permute-start | bytes 1572872 | tf_op jit(solution)/shard_map/ppermute | solution.py:16
  5.1 8.9 %collective-permute-start.1 = (f32[32,2,16,128]{3,0,2,1:T(8,128)S(1)}, f32[32,2,16,128]{3,0,2,1:T(8,128)S(1)}, u32[]{:S(2)}, u32[]{:S(2)}) collective-permute-start(f32[32,2,16,128]{3,0,2,1:T(8,128)S(1)} %copy.81), channel_id=1, source_target_pairs={{32,0},{64,32},{96,64},{128,96},{160,128},{192,160},{224,192},{0,2... | collective-permute-start | bytes 1572872 | tf_op jit(solution)/shard_map/ppermute | solution.py:17
  12.5 15.3 %copy-start.3 = (f32[32,10,16,128]{3,0,2,1:T(8,128)}, f32[32,10,16,128]{3,0,2,1:T(8,128)S(1)}, u32[]{:S(2)}) copy-start(f32[32,10,16,128]{3,0,2,1:T(8,128)S(1)} %get-tuple-element.24) | copy-start | bytes 7864324
  14.1 13.6 %copy-start.2 = (f32[32,10,16,128]{3,0,2,1:T(8,128)}, f32[32,10,16,128]{3,0,2,1:T(8,128)S(1)}, u32[]{:S(2)}) copy-start(f32[32,10,16,128]{3,0,2,1:T(8,128)S(1)} %get-tuple-element.31) | copy-start | bytes 7864324
  14.2 13.6 %copy-start.1 = (f32[32,12,16,128]{3,0,2,1:T(8,128)}, f32[32,12,16,128]{3,0,2,1:T(8,128)S(1)}, u32[]{:S(2)}) copy-start(f32[32,12,16,128]{3,0,2,1:T(8,128)S(1)} %get-tuple-element.32) | copy-start | bytes 9437188
  14.2 13.5 %collective-permute-start.2 = (f32[32,12,2,128]{3,0,2,1:T(8,128)S(1)}, f32[32,12,2,128]{3,0,2,1:T(8,128)S(1)}, u32[]{:S(2)}, u32[]{:S(2)}) collective-permute-start(f32[32,12,2,128]{3,0,2,1:T(8,128)S(1)} %get-tuple-element.20), channel_id=1, source_target_pairs={{0,4},{4,8},{8,12},{12,16},{16,20},{20,24},{24,28},{28,0},{1,5},{5... | collective-permute-start | bytes 1179656 | tf_op jit(solution)/shard_map/ppermute | solution.py:16
  15.6 12.1 %collective-permute-start.3 = (f32[32,12,2,128]{3,0,2,1:T(8,128)S(1)}, f32[32,12,2,128]{3,0,2,1:T(8,128)S(1)}, u32[]{:S(2)}, u32[]{:S(2)}) collective-permute-start(f32[32,12,2,128]{3,0,2,1:T(8,128)S(1)} %get-tuple-element.21), channel_id=1, source_target_pairs={{4,0},{8,4},{12,8},{16,12},{20,16},{24,20},{28,24},{0,28},{5,1},{9... | collective-permute-start | bytes 1179656 | tf_op jit(solution)/shard_map/ppermute | solution.py:17
  36.3 8.1 %collective-permute-start.4 = (f32[32,12,20,2]{0,2,3,1:T(8,128)S(1)}, f32[32,12,20,2]{0,2,3,1:T(8,128)S(1)}, u32[]{:S(2)}, u32[]{:S(2)}) collective-permute-start(f32[32,12,20,2]{0,2,3,1:T(8,128)S(1)} %copy.47), channel_id=1, source_target_pairs={{0,1},{1,2},{2,3},{3,0},{4,5},{5,6},{6,7},{7,4},{8,9},{9,10},{10,1... | collective-permute-start | bytes 184328 | tf_op jit(solution)/shard_map/ppermute | solution.py:16
  41.0 6.7 %collective-permute-start.5 = (f32[32,12,20,2]{0,2,3,1:T(8,128)S(1)}, f32[32,12,20,2]{0,2,3,1:T(8,128)S(1)}, u32[]{:S(2)}, u32[]{:S(2)}) collective-permute-start(f32[32,12,20,2]{0,2,3,1:T(8,128)S(1)} %copy.50), channel_id=1, source_target_pairs={{1,0},{2,1},{3,2},{0,3},{5,4},{6,5},{7,6},{4,7},{9,8},{10,9},{11,1... | collective-permute-start | bytes 184328 | tf_op jit(solution)/shard_map/ppermute | solution.py:17
  47.2 3.3 %copy-start.5 = (f32[8,16,128]{2,1,0:T(8,128)S(1)}, f32[8,16,128]{2,1,0:T(8,128)}, u32[]{:S(2)}) copy-start(f32[8,16,128]{2,1,0:T(8,128)} %param.3) | copy-start | bytes 196612
  67.6 16.8 %copy-start.6 = (f32[8,16,128]{2,1,0:T(8,128)S(1)}, f32[8,16,128]{2,1,0:T(8,128)}, u32[]{:S(2)}) copy-start(f32[8,16,128]{2,1,0:T(8,128)} %param.3) | copy-start | bytes 196612
  67.6 11.5 %collective-permute-start.6 = (f32[32,2,16,128]{3,0,2,1:T(8,128)S(1)}, f32[32,2,16,128]{3,0,2,1:T(8,128)S(1)}, u32[]{:S(2)}, u32[]{:S(2)}) collective-permute-start(f32[32,2,16,128]{3,0,2,1:T(8,128)S(1)} %get-tuple-element.22), channel_id=1, source_target_pairs={{0,32},{32,64},{64,96},{96,128},{128,160},{160,192},{192,224},{224... | collective-permute-start | bytes 1572872 | tf_op jit(solution)/shard_map/ppermute | solution.py:16
  72.9 8.6 %collective-permute-start.7 = (f32[32,2,16,128]{3,0,2,1:T(8,128)S(1)}, f32[32,2,16,128]{3,0,2,1:T(8,128)S(1)}, u32[]{:S(2)}, u32[]{:S(2)}) collective-permute-start(f32[32,2,16,128]{3,0,2,1:T(8,128)S(1)} %get-tuple-element.23), channel_id=1, source_target_pairs={{32,0},{64,32},{96,64},{128,96},{160,128},{192,160},{224,192},{0,2... | collective-permute-start | bytes 1572872 | tf_op jit(solution)/shard_map/ppermute | solution.py:17
  81.6 11.5 %collective-permute-start.8 = (f32[32,12,2,128]{3,0,2,1:T(8,128)S(1)}, f32[32,12,2,128]{3,0,2,1:T(8,128)S(1)}, u32[]{:S(2)}, u32[]{:S(2)}) collective-permute-start(f32[32,12,2,128]{3,0,2,1:T(8,128)S(1)} %get-tuple-element.18), channel_id=1, source_target_pairs={{0,4},{4,8},{8,12},{12,16},{16,20},{20,24},{24,28},{28,0},{1,5},{5... | collective-permute-start | bytes 1179656 | tf_op jit(solution)/shard_map/ppermute | solution.py:16
  81.7 11.4 %collective-permute-start.9 = (f32[32,12,2,128]{3,0,2,1:T(8,128)S(1)}, f32[32,12,2,128]{3,0,2,1:T(8,128)S(1)}, u32[]{:S(2)}, u32[]{:S(2)}) collective-permute-start(f32[32,12,2,128]{3,0,2,1:T(8,128)S(1)} %get-tuple-element.19), channel_id=1, source_target_pairs={{4,0},{8,4},{12,8},{16,12},{20,16},{24,20},{28,24},{0,28},{5,1},{9... | collective-permute-start | bytes 1179656 | tf_op jit(solution)/shard_map/ppermute | solution.py:17
  93.1 0.9 copy-start.4
  106.7 16.2 %collective-permute-start.11 = (f32[32,12,20,2]{0,2,3,1:T(8,128)}, f32[32,12,20,2]{0,2,3,1:T(8,128)}, u32[]{:S(2)}, u32[]{:S(2)}) collective-permute-start(f32[32,12,20,2]{0,2,3,1:T(8,128)} %copy.56), channel_id=1, source_target_pairs={{1,0},{2,1},{3,2},{0,3},{5,4},{6,5},{7,6},{4,7},{9,8},{10,9},{11,1... | collective-permute-start | bytes 184328 | tf_op jit(solution)/shard_map/ppermute | solution.py:17
  109.4 9.8 %collective-permute-start.10 = (f32[32,12,20,2]{0,2,3,1:T(8,128)}, f32[32,12,20,2]{0,2,3,1:T(8,128)}, u32[]{:S(2)}, u32[]{:S(2)}) collective-permute-start(f32[32,12,20,2]{0,2,3,1:T(8,128)} %copy.54), channel_id=1, source_target_pairs={{0,1},{1,2},{2,3},{3,0},{4,5},{5,6},{6,7},{7,4},{8,9},{9,10},{10,1... | collective-permute-start | bytes 184328 | tf_op jit(solution)/shard_map/ppermute | solution.py:16
where the time goes:
time: 231 us
  blocking collectives  76.7 us (33%)
  local copies, waits for them, and re-layouts  47.5 us (21%)
  other arithmetic  39.4 us (17%)
  waiting for transfers between devices  39.1 us (17%)
  starting transfers between devices  22.5 us (10%)
  matrix products  4.81 us (2%)
    psum x1, blocking collectives, per_device(): lower = jnp.linalg.cholesky(lax.psum(correlation, ('gx', 'gy', 'gz')))  76.7 us
    ppermute x6, waiting for transfers between devices, padded_2(): before = lax.ppermute(last, axis, up)  34.6 us
    div x1, other arithmetic, per_device(): (hamiltonian(with_rims(orbitals), potential_cube) - 5.5 * orbitals) / 3.5  17 us
    slice x6, local copies, waits for them, and re-layouts, padded_2(): last = lax.slice_in_dim(x, length - width, length, axis=dim)  16.9 us
    ppermute x6, starting transfers between devices, padded_2(): after = lax.ppermute(leading, axis, down)  11.7 us
    ppermute x6, starting transfers between devices, padded_2(): before = lax.ppermute(last, axis, up)  10.8 us
    sub x1, other arithmetic, per_device(): 2.0 * (hamiltonian(with_rims(first), potential_cube) - 5.5 * first) / 3.5  9.89 us
    slice x3, local copies, waits for them, and re-layouts, padded_2(): leading = lax.slice_in_dim(x, 0, width, axis=dim)  8.68 us
  transfers between devices with their start and end apart: 12, of which 9 were waited for; matrix products, arithmetic and copies ran while one was open for 7% of the time, Pallas kernels for 0%

commit v1 on v0

--- a/solution.py
+++ b/solution.py
@@ -54,7 +54,7 @@
     filtered = second.reshape(norb_count, -1)
     all_cells = filtered.shape[1] * lax.axis_size("gx") * lax.axis_size("gy") * lax.axis_size("gz")
     correlation = jnp.dot(filtered, filtered.T, precision=lax.Precision.HIGHEST) / all_cells
-    lower = jnp.linalg.cholesky(lax.psum(correlation, ("gx", "gy", "gz")))
+    lower = jnp.linalg.cholesky(jnp.sum(lax.all_gather(correlation, ("gx", "gy", "gz")), axis=0))
     basis = jax.scipy.linalg.solve_triangular(lower, filtered, lower=True)
     return (basis.reshape(orbitals.shape), lower.T)
 

time: 231 us -> 284 us (1.23)
  waiting for transfers between devices: 39.1 us -> 149 us
  blocking collectives: 76.7 us -> 0 us
  between operations: 0.85 us -> 14.2 us
  other arithmetic: 39.4 us -> 42.7 us
  local copies, waits for them, and re-layouts: 47.5 us -> 50.4 us
    all_gather x0 -> x1, waiting for transfers between devices: none -> 110 us  [per_device(): lax.all_gather(correlation, ('gx', 'gy', 'gz'))]
    psum x1 -> x0, blocking collectives: 76.7 us -> none  [per_device(): lower = jnp.linalg.cholesky(lax.psum(correlation, ('gx', 'gy', 'gz')))]
    unnamed x21 -> x23, local copies, waits for them, and re-layouts: 6 us -> 7.3 us
  transfers between devices with their start and end apart: 12 -> 13, of which waited for: 9 -> 10; matrix products, arithmetic and copies ran while one was open for 7% -> 7% of each run, Pallas kernels for 0% -> 0%
where the time goes in v1:
time: 284 us
  waiting for transfers between devices  149 us (52%)
  local copies, waits for them, and re-layouts  50.4 us (18%)
  other arithmetic  42.7 us (15%)
  starting transfers between devices  22.6 us (8%)
  between operations  14.2 us (5%)
  matrix products  5.42 us (2%)
    all_gather x1, waiting for transfers between devices, per_device(): lax.all_gather(correlation, ('gx', 'gy', 'gz'))  110 us
    ppermute x6, waiting for transfers between devices, padded_2(): before = lax.ppermute(last, axis, up)  34.5 us
    div x1, other arithmetic, per_device(): (hamiltonian(with_rims(orbitals), potential_cube) - 5.5 * orbitals) / 3.5  17.4 us
    slice x6, local copies, waits for them, and re-layouts, padded_2(): last = lax.slice_in_dim(x, length - width, length, axis=dim)  16.9 us
    ppermute x6, starting transfers between devices, padded_2(): after = lax.ppermute(leading, axis, down)  11.7 us
    ppermute x6, starting transfers between devices, padded_2(): before = lax.ppermute(last, axis, up)  10.8 us
    sub x1, other arithmetic, per_device(): 2.0 * (hamiltonian(with_rims(first), potential_cube) - 5.5 * first) / 3.5  10.3 us
    slice x3, local copies, waits for them, and re-layouts, padded_2(): leading = lax.slice_in_dim(x, 0, width, axis=dim)  8.68 us
  transfers between devices with their start and end apart: 13, of which 10 were waited for; matrix products, arithmetic and copies ran while one was open for 7% of the time, Pallas kernels for 0%

profile of v1, /device:TPU:1, one launch (start us, length us, event | category | flops | bytes accessed | tf_op | source)
XLA Modules:
  0.0 284.0 jit_solution(16003422079930115617)
XLA Ops:
  8.8 2.6 collective-permute-start
  12.4 5.2 %collective-permute-done = f32[32,2,16,128]{3,0,2,1:T(8,128)S(1)} collective-permute-done((f32[32,2,16,128]{3,0,2,1:T(8,128)S(1)}, f32[32,2,16,128]{3,0,2,1:T(8,128)S(1)}, u32[]{:S(2)}, u32[]{:S(2)}) %collective-permute-start) | collective-permute-done | bytes 524320 | tf_op jit(solution)/shard_map/ppermute | solution.py:16
  22.2 4.0 %collective-permute-start.3 = (f32[32,12,2,128]{3,0,2,1:T(8,128)S(1)}, f32[32,12,2,128]{3,0,2,1:T(8,128)S(1)}, u32[]{:S(2)}, u32[]{:S(2)}) collective-permute-start(f32[32,12,2,128]{3,0,2,1:T(8,128)S(1)} %get-tuple-element.21), channel_id=1, source_target_pairs={{4,0},{8,4},{12,8},{16,12},{20,16},{24,20},{28,24},{0,28},{5,1},{9... | collective-permute-start | bytes 1179656 | tf_op jit(solution)/shard_map/ppermute | solution.py:17
  26.3 8.1 %collective-permute-done.2 = f32[32,12,2,128]{3,0,2,1:T(8,128)S(1)} collective-permute-done((f32[32,12,2,128]{3,0,2,1:T(8,128)S(1)}, f32[32,12,2,128]{3,0,2,1:T(8,128)S(1)}, u32[]{:S(2)}, u32[]{:S(2)}) %collective-permute-start.2) | collective-permute-done | bytes 393248 | tf_op jit(solution)/shard_map/ppermute | solution.py:16
  34.8 4.7 %fusion.56 = (f32[32,12,20,2]{3,0,2,1:T(8,128)}, f32[32,12,20,2]{3,0,2,1:T(8,128)}) fusion(f32[32,12,20,128]{3,0,2,1:T(8,128)S(1)} %pad_maximum_fusion), kind=kLoop, calls=%fused_computation.120 | loop fusion | bytes 245760 | tf_op jit(solution)/shard_map/slice | solution.py:14
  39.5 3.4 %copy.44 = f32[32,12,20,2]{0,2,3,1:T(8,128)S(1)} copy(f32[32,12,20,2]{3,0,2,1:T(8,128)} %get-tuple-element.14) | data formatting | bytes 122880 | tf_op jit(solution)/shard_map/slice | solution.py:14
  44.2 3.4 %copy.47 = f32[32,12,20,2]{0,2,3,1:T(8,128)S(1)} copy(f32[32,12,20,2]{3,0,2,1:T(8,128)} %get-tuple-element.15) | data formatting | bytes 122880 | tf_op jit(solution)/shard_map/slice | solution.py:15
  50.9 2.9 %copy.45 = f32[32,12,20,2]{3,0,2,1:T(8,128)} copy(f32[32,12,20,2]{0,2,3,1:T(8,128)S(1)} %collective-permute-done.4) | data formatting | bytes 122880 | tf_op jit(solution)/shard_map/ppermute | solution.py:16
  54.2 2.9 %copy.48 = f32[32,12,20,2]{3,0,2,1:T(8,128)} copy(f32[32,12,20,2]{0,2,3,1:T(8,128)S(1)} %collective-permute-done.5) | data formatting | bytes 122880 | tf_op jit(solution)/shard_map/ppermute | solution.py:17
  57.1 17.4 %broadcast_multiply_fusion = (f32[32,8,16,128]{3,0,2,1:T(8,128)S(1)}, f32[32,8,16,128]{3,0,2,1:T(8,128)}) fusion(f32[8,16,128]{2,1,0:T(8,128)S(1)} %copy-done.6, f32[32,12,20,2]{3,0,2,1:T(8,128)} %copy.48, f32[32,12,2,128]{3,0,2,1:T(8,128)S(1)} %collective-permute-done.3, f32[32,12,16,128]{3,0,2,1:T(8,128)} %copy-done.2, ...), kind=kLoop, calls=%fused_computation.97 | loop fusion | flops 24641536 | bytes 18800640 | tf_op jit(solution)/shard_map/div | solution.py:51
  74.6 5.3 %collective-permute-start.6 = (f32[32,2,16,128]{3,0,2,1:T(8,128)S(1)}, f32[32,2,16,128]{3,0,2,1:T(8,128)S(1)}, u32[]{:S(2)}, u32[]{:S(2)}) collective-permute-start(f32[32,2,16,128]{3,0,2,1:T(8,128)S(1)} %get-tuple-element.22), channel_id=1, source_target_pairs={{0,32},{32,64},{64,96},{96,128},{128,160},{160,192},{192,224},{224... | collective-permute-start | bytes 1572872 | tf_op jit(solution)/shard_map/ppermute | solution.py:16
  79.9 6.1 %collective-permute-done.6 = f32[32,2,16,128]{3,0,2,1:T(8,128)S(1)} collective-permute-done((f32[32,2,16,128]{3,0,2,1:T(8,128)S(1)}, f32[32,2,16,128]{3,0,2,1:T(8,128)S(1)}, u32[]{:S(2)}, u32[]{:S(2)}) %collective-permute-start.6) | collective-permute-done | bytes 524320 | tf_op jit(solution)/shard_map/ppermute | solution.py:16
  86.1 2.5 collective-permute-done.7
  88.7 2.7 collective-permute-start.9
  92.0 8.1 %collective-permute-done.8 = f32[32,12,2,128]{3,0,2,1:T(8,128)S(1)} collective-permute-done((f32[32,12,2,128]{3,0,2,1:T(8,128)S(1)}, f32[32,12,2,128]{3,0,2,1:T(8,128)S(1)}, u32[]{:S(2)}, u32[]{:S(2)}) %collective-permute-start.8) | collective-permute-done | bytes 393248 | tf_op jit(solution)/shard_map/ppermute | solution.py:16
  100.9 4.7 %fusion.55 = (f32[32,12,20,2]{3,0,2,1:T(8,128)}, f32[32,12,20,2]{3,0,2,1:T(8,128)}) fusion(f32[32,12,20,128]{3,0,2,1:T(8,128)S(1)} %pad_maximum_fusion.1), kind=kLoop, calls=%fused_computation.119 | loop fusion | bytes 245760 | tf_op jit(solution)/shard_map/slice | solution.py:14
  105.6 4.0 %copy.51 = f32[32,12,20,2]{0,2,3,1:T(8,128)} copy(f32[32,12,20,2]{3,0,2,1:T(8,128)} %get-tuple-element.12) | data formatting | bytes 122880 | tf_op jit(solution)/shard_map/slice | solution.py:14
  109.6 4.0 %copy.53 = f32[32,12,20,2]{0,2,3,1:T(8,128)} copy(f32[32,12,20,2]{3,0,2,1:T(8,128)} %get-tuple-element.13) | data formatting | bytes 122880 | tf_op jit(solution)/shard_map/slice | solution.py:15
  113.7 2.7 collective-permute-start.11
  116.3 4.3 %maximum_maximum_fusion = (f32[32,12,18,128]{3,0,2,1:T(8,128)}, f32[32,12,18,128]{3,0,2,1:T(8,128)}) fusion(f32[32,2,16,128]{3,0,2,1:T(8,128)S(1)} %collective-permute-done.7, f32[32,8,16,128]{3,0,2,1:T(8,128)S(1)} %get-tuple-element.10, f32[32,2,16,128]{3,0,2,1:T(8,128)S(1)} %collective-permute-done.6, f32[32,12,2,128]{3,0,2,1:T(8,128)S(1)} %collective-permute-done.8, ...), kind=kLoop, calls=%fused_computation.6 | loop fusion | flops 5308416 | bytes 11010048 | tf_op jit(solution)/shard_map/concatenate | solution.py:18
  120.7 5.4 %collective-permute-done.10 = f32[32,12,20,2]{0,2,3,1:T(8,128)} collective-permute-done((f32[32,12,20,2]{0,2,3,1:T(8,128)}, f32[32,12,20,2]{0,2,3,1:T(8,128)}, u32[]{:S(2)}, u32[]{:S(2)}) %collective-permute-start.10) | collective-permute-done | bytes 61472 | tf_op jit(solution)/shard_map/ppermute | solution.py:16
  126.1 3.8 %copy.52 = f32[32,12,20,2]{3,0,2,1:T(8,128)} copy(f32[32,12,20,2]{0,2,3,1:T(8,128)} %collective-permute-done.10) | data formatting | bytes 122880 | tf_op jit(solution)/shard_map/ppermute | solution.py:16
  129.8 3.8 %copy.54 = f32[32,12,20,2]{3,0,2,1:T(8,128)} copy(f32[32,12,20,2]{0,2,3,1:T(8,128)} %collective-permute-done.11) | data formatting | bytes 122880 | tf_op jit(solution)/shard_map/ppermute | solution.py:17
  133.6 10.3 %fusion.12 = f32[32,8,16,128]{3,0,2,1:T(8,128)S(1)} fusion(f32[32,8,16,128]{3,0,2,1:T(8,128)S(1)} %get-tuple-element.10, f32[32,2,16,128]{3,0,2,1:T(8,128)S(1)} %collective-permute-done.7, f32[32,2,16,128]{3,0,2,1:T(8,128)S(1)} %collective-permute-done.6, f32[32,12,20,2]{3,0,2,1:T(8,128)} %copy.54, f32[32,12,2,128]{3,0,2,1:T(8,128)} %copy-done.5, ...), kind=kLoop, calls=%fused_computation.24 | loop fusion | flops 29360128 | bytes 18800640 | tf_op jit(solution)/shard_map/sub | solution.py:52
  145.2 2.4 fusion.50
  147.6 2.8 copy.57
  152.0 109.5 %all-gather.3.cloned.1.call-done = f32[8192,32]{1,0:T(8,128)} async-done(((f32[32,32]{1,0:T(8,128)}), f32[8192,32]{1,0:T(8,128)}) %all-gather.3.cloned.1.call-update) | async-done | bytes 1048592 | tf_op jit(solution)/shard_map/all_gather | solution.py:57
  261.6 2.5 reduce_sum.9
  264.2 2.9 %cholesky.16 = f32[32,32]{1,0:T(8,128)S(1)} custom-call(f32[32,32]{1,0:T(8,128)S(1)} %fusion.52), custom_call_target="Cholesky" | custom-call | tf_op jit(solution)/shard_map/jit(cholesky)/cholesky | solution.py:57
  269.1 2.4 custom-call.7
  271.5 3.0 %fusion.48 = f32[32,8,16,128]{3,0,2,1:T(8,128)S(1)} fusion(f32[8,16,128,32]{2,1,0,3:T(8,128)S(1)} %bitcast.35, f32[1,32,32]{1,2,0:T(8,128)S(1)} %custom-call.7), kind=kOutput, calls=%fused_computation.93 | convolution fusion | flops 201326592 | bytes 4198400 | tf_op jit(solution)/shard_map/jit(_solve_triangular)/triangular_solve | solution.py:58
  274.6 2.5 copy.60
  (51 shorter events, 19.5 us)
Async XLA Ops:
  7.2 254.4 %all-gather.3.cloned.1.call-start = ((), (), s32[]{:S(2)}) async-start(), calls=%async_computation | async-start | bytes 4210688 | tf_op jit(solution)/shard_map/all_gather | solution.py:57
  8.5 9.2 %copy-start.1 = (f32[32,8,16,128]{3,2,1,0:T(8,128)S(1)}, f32[32,8,16,128]{3,2,1,0:T(8,128)}, u32[]{:S(2)}) copy-start(f32[32,8,16,128]{3,2,1,0:T(8,128)} %param.2) | copy-start | bytes 6291460
  8.8 8.7 %collective-permute-start = (f32[32,2,16,128]{3,0,2,1:T(8,128)S(1)}, f32[32,2,16,128]{3,0,2,1:T(8,128)S(1)}, u32[]{:S(2)}, u32[]{:S(2)}) collective-permute-start(f32[32,2,16,128]{3,0,2,1:T(8,128)S(1)} %copy.75), channel_id=1, source_target_pairs={{0,32},{32,64},{64,96},{96,128},{128,160},{160,192},{192,224},{224... | collective-permute-start | bytes 1572872 | tf_op jit(solution)/shard_map/ppermute | solution.py:16
  11.7 8.9 %collective-permute-start.1 = (f32[32,2,16,128]{3,0,2,1:T(8,128)S(1)}, f32[32,2,16,128]{3,0,2,1:T(8,128)S(1)}, u32[]{:S(2)}, u32[]{:S(2)}) collective-permute-start(f32[32,2,16,128]{3,0,2,1:T(8,128)S(1)} %copy.76), channel_id=1, source_target_pairs={{32,0},{64,32},{96,64},{128,96},{160,128},{192,160},{224,192},{0,2... | collective-permute-start | bytes 1572872 | tf_op jit(solution)/shard_map/ppermute | solution.py:17
  19.0 15.3 %copy-start.4 = (f32[32,10,16,128]{3,0,2,1:T(8,128)}, f32[32,10,16,128]{3,0,2,1:T(8,128)S(1)}, u32[]{:S(2)}) copy-start(f32[32,10,16,128]{3,0,2,1:T(8,128)S(1)} %get-tuple-element.24) | copy-start | bytes 7864324
  20.7 13.6 %copy-start.3 = (f32[32,10,16,128]{3,0,2,1:T(8,128)}, f32[32,10,16,128]{3,0,2,1:T(8,128)S(1)}, u32[]{:S(2)}) copy-start(f32[32,10,16,128]{3,0,2,1:T(8,128)S(1)} %get-tuple-element.31) | copy-start | bytes 7864324
  20.7 13.6 %copy-start.2 = (f32[32,12,16,128]{3,0,2,1:T(8,128)}, f32[32,12,16,128]{3,0,2,1:T(8,128)S(1)}, u32[]{:S(2)}) copy-start(f32[32,12,16,128]{3,0,2,1:T(8,128)S(1)} %get-tuple-element.32) | copy-start | bytes 9437188
  20.8 13.5 %collective-permute-start.2 = (f32[32,12,2,128]{3,0,2,1:T(8,128)S(1)}, f32[32,12,2,128]{3,0,2,1:T(8,128)S(1)}, u32[]{:S(2)}, u32[]{:S(2)}) collective-permute-start(f32[32,12,2,128]{3,0,2,1:T(8,128)S(1)} %get-tuple-element.20), channel_id=1, source_target_pairs={{0,4},{4,8},{8,12},{12,16},{16,20},{20,24},{24,28},{28,0},{1,5},{5... | collective-permute-start | bytes 1179656 | tf_op jit(solution)/shard_map/ppermute | solution.py:16
  22.2 12.1 %collective-permute-start.3 = (f32[32,12,2,128]{3,0,2,1:T(8,128)S(1)}, f32[32,12,2,128]{3,0,2,1:T(8,128)S(1)}, u32[]{:S(2)}, u32[]{:S(2)}) collective-permute-start(f32[32,12,2,128]{3,0,2,1:T(8,128)S(1)} %get-tuple-element.21), channel_id=1, source_target_pairs={{4,0},{8,4},{12,8},{16,12},{20,16},{24,20},{28,24},{0,28},{5,1},{9... | collective-permute-start | bytes 1179656 | tf_op jit(solution)/shard_map/ppermute | solution.py:17
  42.8 8.1 %collective-permute-start.4 = (f32[32,12,20,2]{0,2,3,1:T(8,128)S(1)}, f32[32,12,20,2]{0,2,3,1:T(8,128)S(1)}, u32[]{:S(2)}, u32[]{:S(2)}) collective-permute-start(f32[32,12,20,2]{0,2,3,1:T(8,128)S(1)} %copy.44), channel_id=1, source_target_pairs={{0,1},{1,2},{2,3},{3,0},{4,5},{5,6},{6,7},{7,4},{8,9},{9,10},{10,1... | collective-permute-start | bytes 184328 | tf_op jit(solution)/shard_map/ppermute | solution.py:16
  47.6 6.7 %collective-permute-start.5 = (f32[32,12,20,2]{0,2,3,1:T(8,128)S(1)}, f32[32,12,20,2]{0,2,3,1:T(8,128)S(1)}, u32[]{:S(2)}, u32[]{:S(2)}) collective-permute-start(f32[32,12,20,2]{0,2,3,1:T(8,128)S(1)} %copy.47), channel_id=1, source_target_pairs={{1,0},{2,1},{3,2},{0,3},{5,4},{6,5},{7,6},{4,7},{9,8},{10,9},{11,1... | collective-permute-start | bytes 184328 | tf_op jit(solution)/shard_map/ppermute | solution.py:17
  53.8 3.3 %copy-start.6 = (f32[8,16,128]{2,1,0:T(8,128)S(1)}, f32[8,16,128]{2,1,0:T(8,128)}, u32[]{:S(2)}) copy-start(f32[8,16,128]{2,1,0:T(8,128)} %param.3) | copy-start | bytes 196612
  74.6 16.8 %copy-start.7 = (f32[8,16,128]{2,1,0:T(8,128)S(1)}, f32[8,16,128]{2,1,0:T(8,128)}, u32[]{:S(2)}) copy-start(f32[8,16,128]{2,1,0:T(8,128)} %param.3) | copy-start | bytes 196612
  74.6 11.5 %collective-permute-start.6 = (f32[32,2,16,128]{3,0,2,1:T(8,128)S(1)}, f32[32,2,16,128]{3,0,2,1:T(8,128)S(1)}, u32[]{:S(2)}, u32[]{:S(2)}) collective-permute-start(f32[32,2,16,128]{3,0,2,1:T(8,128)S(1)} %get-tuple-element.22), channel_id=1, source_target_pairs={{0,32},{32,64},{64,96},{96,128},{128,160},{160,192},{192,224},{224... | collective-permute-start | bytes 1572872 | tf_op jit(solution)/shard_map/ppermute | solution.py:16
  79.9 8.6 %collective-permute-start.7 = (f32[32,2,16,128]{3,0,2,1:T(8,128)S(1)}, f32[32,2,16,128]{3,0,2,1:T(8,128)S(1)}, u32[]{:S(2)}, u32[]{:S(2)}) collective-permute-start(f32[32,2,16,128]{3,0,2,1:T(8,128)S(1)} %get-tuple-element.23), channel_id=1, source_target_pairs={{32,0},{64,32},{96,64},{128,96},{160,128},{192,160},{224,192},{0,2... | collective-permute-start | bytes 1572872 | tf_op jit(solution)/shard_map/ppermute | solution.py:17
  88.6 11.5 %collective-permute-start.8 = (f32[32,12,2,128]{3,0,2,1:T(8,128)S(1)}, f32[32,12,2,128]{3,0,2,1:T(8,128)S(1)}, u32[]{:S(2)}, u32[]{:S(2)}) collective-permute-start(f32[32,12,2,128]{3,0,2,1:T(8,128)S(1)} %get-tuple-element.18), channel_id=1, source_target_pairs={{0,4},{4,8},{8,12},{12,16},{16,20},{20,24},{24,28},{28,0},{1,5},{5... | collective-permute-start | bytes 1179656 | tf_op jit(solution)/shard_map/ppermute | solution.py:16
  88.7 11.4 %collective-permute-start.9 = (f32[32,12,2,128]{3,0,2,1:T(8,128)S(1)}, f32[32,12,2,128]{3,0,2,1:T(8,128)S(1)}, u32[]{:S(2)}, u32[]{:S(2)}) collective-permute-start(f32[32,12,2,128]{3,0,2,1:T(8,128)S(1)} %get-tuple-element.19), channel_id=1, source_target_pairs={{4,0},{8,4},{12,8},{16,12},{20,16},{24,20},{28,24},{0,28},{5,1},{9... | collective-permute-start | bytes 1179656 | tf_op jit(solution)/shard_map/ppermute | solution.py:17
  100.1 0.8 copy-start.5
  113.7 16.2 %collective-permute-start.11 = (f32[32,12,20,2]{0,2,3,1:T(8,128)}, f32[32,12,20,2]{0,2,3,1:T(8,128)}, u32[]{:S(2)}, u32[]{:S(2)}) collective-permute-start(f32[32,12,20,2]{0,2,3,1:T(8,128)} %copy.53), channel_id=1, source_target_pairs={{1,0},{2,1},{3,2},{0,3},{5,4},{6,5},{7,6},{4,7},{9,8},{10,9},{11,1... | collective-permute-start | bytes 184328 | tf_op jit(solution)/shard_map/ppermute | solution.py:17
  116.3 9.8 %collective-permute-start.10 = (f32[32,12,20,2]{0,2,3,1:T(8,128)}, f32[32,12,20,2]{0,2,3,1:T(8,128)}, u32[]{:S(2)}, u32[]{:S(2)}) collective-permute-start(f32[32,12,20,2]{0,2,3,1:T(8,128)} %copy.51), channel_id=1, source_target_pairs={{0,1},{1,2},{2,3},{3,0},{4,5},{5,6},{6,7},{7,4},{8,9},{9,10},{10,1... | collective-permute-start | bytes 184328 | tf_op jit(solution)/shard_map/ppermute | solution.py:16
  143.9 1.3 copy-start
Sparse Core Ops, SparseCore 0:
  147.7 113.7 all-gather.2
